TPU v7x, 256 devices: a whole 4x4x8 slice. The times are simulated.
256 devices in a mesh: slab: 64 (over z_hi, x, y), rep: 4 (over z_lo, core).
Axes of the slice: x: 4, y: 4, z: 8 (z_hi: 4, z_lo: 2; z = z_hi * 2 + z_lo), core: 2. Of those that a mesh axis runs over, the one named last changes fastest.
Arguments:
- volume: float32 [2048, 128, 1024], P('slab', 'rep'), may hold values from -6 to 6
- slices_x: bfloat16 [2048, 128, 128], P('slab', 'rep'), may hold values from -6 to 6
- slices_y: bfloat16 [2048, 16, 1024], P('slab'), may hold values from -6 to 6
- slices_z: bfloat16 [256, 128, 1024], P('slab', 'rep'), may hold values from -6 to 6
- profiles: float32 [4, 16, 128], replicated, may hold values from -1 to 2
- profile_index: int32 [25], replicated, may hold values from 0 to 3
- block_shift: int32 [25], replicated, may hold values from 0 to 7
Outputs:
- updated: float32 [2048, 128, 1024], P('slab', 'rep')
All inputs are finite; a program needn't handle non-finite values.
Results may differ from a plain program's by a relative error of at most 0.0044.
Values may be sent and summed in bfloat16 or wider, within the bound.
No kernel may reach another device: no remote copies, remote signals or barrier semaphores. Data moves between devices by JAX's collectives and lax.ppermute only.
A program may use at most 64 MiB of HBM per device.

v0:
```python
import jax
import jax.numpy as jnp
from jax import lax
from jax.sharding import Mesh, PartitionSpec as P

BLOCK = 128
SLICES = 16
step_size = 0.5


def block_mats(profiles, profile_index, block_shift):
    kinds = profiles.shape[0]
    span = profiles.shape[2]
    onehot = (profile_index[:, None] == jnp.arange(kinds, dtype=jnp.int32)[None, :]).astype(
        jnp.float32
    )
    picked = jnp.einsum("bk,ksl->bsl", onehot, profiles, precision=lax.Precision.HIGHEST)
    columns = jnp.arange(span, dtype=jnp.int32)
    target = (columns[None, :] + block_shift[:, None]) % span
    moving = (target[:, :, None] == columns[None, None, :]).astype(jnp.float32)
    shifted = jnp.einsum("bsj,bjl->bsl", picked, moving, precision=lax.Precision.HIGHEST)
    return shifted.astype(jnp.bfloat16)


def banded_matrix(along):
    count = along.shape[0]
    identity = jnp.eye(count, dtype=jnp.bfloat16)
    return (along[:, :, None, :] * identity[:, None, :, None]).reshape(
        count * SLICES, count * BLOCK
    )


def shards(volume, slices_x, slices_y, slices_z, profiles, profile_index, block_shift):
    planes, rows_here, width = volume.shape
    count_x = width // BLOCK
    count_y = slices_y.shape[1] // SLICES
    mats = block_mats(profiles, profile_index, block_shift)
    along_x = mats[:count_x]
    along_y = mats[count_x : count_x + count_y]
    along_z = mats[count_x + count_y :]
    coarse = volume.astype(jnp.bfloat16)
    banded_x = banded_matrix(along_x)
    flat_coarse = coarse.reshape(planes * rows_here, width)
    fwd_x = lax.dot_general(
        flat_coarse, banded_x, (((1,), (1,)), ((), ())), preferred_element_type=jnp.float32
    )
    resid_x = (
        slices_x.reshape(planes * rows_here, count_x * SLICES).astype(jnp.float32) - fwd_x
    ).astype(jnp.bfloat16)
    corr_x = jnp.dot(resid_x, banded_x, preferred_element_type=jnp.float32).reshape(
        planes, rows_here, width
    )
    rep = lax.axis_index("rep")
    nrep = lax.axis_size("rep")
    band_y = lax.dynamic_slice_in_dim(along_y[0], rep * rows_here, rows_here, 1)
    partial_y = jnp.einsum("sl,zlx->zsx", band_y, coarse, preferred_element_type=jnp.float32)
    fwd_y = lax.psum_scatter(partial_y, "rep", scatter_dimension=0, tiled=True)
    part_z = planes // nrep
    obs_y = lax.dynamic_slice_in_dim(slices_y, rep * part_z, part_z, 0)
    resid_y = (obs_y.astype(jnp.float32) - fwd_y).astype(jnp.bfloat16)
    resid_y = lax.all_gather(resid_y, "rep", axis=0, tiled=True)
    corr_y = jnp.einsum("sl,zsx->zlx", band_y, resid_y, preferred_element_type=jnp.float32)
    zb = lax.axis_index("zb")
    zq = lax.axis_index("zq")
    mat_z = lax.dynamic_index_in_dim(along_z, zb, 0, keepdims=False)
    band_z = lax.dynamic_slice_in_dim(mat_z, zq * planes, planes, 1)
    partial_z = jnp.einsum("sl,lyx->syx", band_z, coarse, preferred_element_type=jnp.float32)
    fwd_z = lax.psum_scatter(partial_z, "zq", scatter_dimension=0, tiled=True)
    resid_z = (slices_z.astype(jnp.float32) - fwd_z).astype(jnp.bfloat16)
    resid_z = lax.all_gather(resid_z, "zq", axis=0, tiled=True)
    corr_z = jnp.einsum("sl,syx->lyx", band_z, resid_z, preferred_element_type=jnp.float32)
    return volume + step_size * (corr_x + corr_y + corr_z)


def solution(mesh):
    nslab, nrep = mesh.devices.shape
    slab = ("zb", "zq")

    def run(volume, *rest):
        group = BLOCK // (volume.shape[0] // nslab)
        inner = Mesh(mesh.devices.reshape(nslab // group, group, nrep), ("zb", "zq", "rep"))
        return jax.shard_map(
            shards,
            mesh=inner,
            in_specs=(
                P(slab, "rep", None),
                P(slab, "rep", None),
                P(slab, None, None),
                P(slab, "rep", None),
                P(),
                P(),
                P(),
            ),
            out_specs=P(slab, "rep", None),
            check_vma=False,
        )(volume, *rest)

    return run
```

profile of v0, /device:TPU:1, one launch (start us, length us, event | category | flops | bytes accessed | tf_op | source)
XLA Modules:
  0.0 158.2 jit_solution(11104190824409723244)
XLA Ops:
  6.5 0.7 add_select_fusion
  7.3 1.0 fusion.15
  8.3 1.0 fusion.8
  9.3 2.5 %convert_element_type.40 = bf16[32,32,1024]{2,1,0:T(8,128)(2,1)S(1)} convert(f32[32,32,1024]{2,1,0:T(8,128)} %param.7) | non-fusion elementwise | flops 1048576 | bytes 6291456 | tf_op jit(solution)/shard_map/convert_element_type | solution.py:41
  11.9 2.4 %fusion.3 = f32[16,32,1024]{2,0,1:T(8,128)S(1)} fusion(bf16[32,32,1024]{2,1,0:T(8,128)(2,1)S(1)} %convert_element_type.40, bf16[16,16,128]{2,1,0:T(8,128)(2,1)S(1)} %slice.14, s32[]{:T(128)S(6)} %select_n.32, s32[]{:T(128)S(6)} %select_n.34), kind=kOutput, calls=%fused_computation.4 | convolution fusion | flops 33554432 | bytes 4198408 | tf_op jit(solution)/shard_map/sl,lyx->syx/dot_general | solution.py:67
  14.2 2.5 %copy.21 = f32[16,32,1024]{2,1,0:T(8,128)} copy(f32[16,32,1024]{2,0,1:T(8,128)S(1)} %fusion.3) | data formatting | bytes 4194304 | tf_op jit(solution)/shard_map/sl,lyx->syx/dot_general | solution.py:67
  16.8 0.0 reduce-scatter.3.cloned.1.call-start
  16.9 1.8 %convolution_bitcast_fusion = f32[32,16,1024]{2,1,0:T(8,128)} fusion(bf16[32,32,1024]{2,1,0:T(8,128)(2,1)S(1)} %convert_element_type.40, bf16[1,16,128]{2,1,0:T(8,128)(2,1)S(1)} %slice.13, s32[]{:T(128)S(6)} %select_n.30), kind=kOutput, calls=%fused_computation.8 | convolution fusion | flops 33554432 | bytes 4198404 | tf_op jit(solution)/shard_map/sl,zlx->zsx/dot_general | solution.py:56
  18.8 34.2 %reduce-scatter.5.cloned.1.call-done = f32[4,32,1024]{2,1,0:T(8,128)} async-done(((f32[16,32,1024]{2,1,0:T(8,128)}), f32[4,32,1024]{2,1,0:T(8,128)}) %reduce-scatter.5.cloned.1.call-update) | async-done | bytes 524304 | tf_op jit(solution)/shard_map/reduce_scatter | solution.py:68
  53.0 1.8 %subtract_convert_fusion = bf16[4,32,1024]{2,1,0:T(8,128)(2,1)} fusion(f32[4,32,1024]{2,1,0:T(8,128)} %reduce-scatter.5.cloned.1.call-done, bf16[4,32,1024]{2,1,0:T(8,128)(2,1)S(1)} %copy-done.3), kind=kLoop, calls=%fused_computation.16 | loop fusion | flops 393216 | bytes 1048576 | tf_op jit(solution)/shard_map/convert_element_type | solution.py:69
  54.8 0.2 all-gather.3.cloned.1.call-start
  55.1 31.4 %reduce-scatter.3.cloned.1.call-done = f32[8,16,1024]{2,1,0:T(8,128)} async-done(((f32[32,16,1024]{2,1,0:T(8,128)}), f32[8,16,1024]{2,1,0:T(8,128)}) %reduce-scatter.3.cloned.1.call-update) | async-done | bytes 524304 | tf_op jit(solution)/shard_map/reduce_scatter | solution.py:57
  86.4 1.9 %subtract_convert_fusion.1 = bf16[8,16,1024]{2,1,0:T(8,128)(2,1)} fusion(f32[8,16,1024]{2,1,0:T(8,128)} %reduce-scatter.3.cloned.1.call-done, bf16[32,16,1024]{2,1,0:T(8,128)(2,1)} %param.9, s32[]{:T(128)S(6)} %select_n.29), kind=kLoop, calls=%fused_computation.17 | loop fusion | flops 393216 | bytes 1048580 | tf_op jit(solution)/shard_map/convert_element_type | solution.py:60
  88.3 0.1 broadcast_multiply_fusion
  88.4 0.8 reshape.72
  89.2 0.1 bitcast_convert_fusion
  89.3 0.2 copy.18
  89.5 0.8 fusion.7
  90.4 0.2 copy.19
  90.5 2.7 %fusion.37 = f32[32,32,1024]{2,1,0:T(8,128)} fusion(bf16[32,32,128]{2,1,0:T(8,128)(2,1)S(1)} %bitcast.50, bf16[128,1024,1]{1,0,2:T(8,128)(2,1)S(1)} %copy-done.1), kind=kOutput, calls=%fused_computation.49 | convolution fusion | flops 268435456 | bytes 4718592 | tf_op jit(solution)/shard_map/dot_general | solution.py:50
  93.2 19.7 %all-gather.5.cloned.1.call-done = bf16[16,32,1024]{2,1,0:T(8,128)(2,1)} async-done(((bf16[4,32,1024]{2,1,0:T(8,128)(2,1)}), bf16[16,32,1024]{2,1,0:T(8,128)(2,1)}) %all-gather.5.cloned.1.call-update) | async-done | bytes 1048592 | tf_op jit(solution)/shard_map/all_gather | solution.py:70
  112.9 4.1 %fusion.9 = f32[32,32,1024]{2,0,1:T(8,128)} fusion(bf16[16,32,1024]{2,1,0:T(8,128)(2,1)} %all-gather.5.cloned.1.call-done, bf16[16,16,128]{2,1,0:T(8,128)(2,1)S(1)} %slice.14, s32[]{:T(128)S(6)} %select_n.32, s32[]{:T(128)S(6)} %select_n.34), kind=kOutput, calls=%fused_computation.13 | convolution fusion | flops 33554432 | bytes 5246984 | tf_op jit(solution)/shard_map/sl,syx->lyx/dot_general | solution.py:71
  117.1 23.7 %all-gather.3.cloned.1.call-done = bf16[32,16,1024]{2,1,0:T(8,128)(2,1)} async-done(((bf16[8,16,1024]{2,1,0:T(8,128)(2,1)}), bf16[32,16,1024]{2,1,0:T(8,128)(2,1)}) %all-gather.3.cloned.1.call-update) | async-done | bytes 1048592 | tf_op jit(solution)/shard_map/all_gather | solution.py:61
  140.8 10.9 %fusion.2 = f32[32,32,1024]{2,1,0:T(8,128)} fusion(f32[32,32,1024]{2,1,0:T(8,128)} %param.7, f32[32,32,1024]{2,1,0:T(8,128)} %fusion.37, f32[32,32,1024]{2,0,1:T(8,128)} %fusion.9, bf16[32,16,1024]{2,1,0:T(8,128)(2,1)} %all-gather.3.cloned.1.call-done, bf16[1,16,128]{2,1,0:T(8,128)(2,1)S(1)} %slice.13, s32[]{:T(128)S(6)} %select_n.30), kind=kOutput, calls=%fused_computation.3 | convolution fusion | flops 37748736 | bytes 17829892 | tf_op jit(solution)/shard_map/sl,zsx->zlx/dot_general | solution.py:62
  (18 shorter events, 0.2 us)
Async XLA Ops:
  6.5 0.8 copy-start
  6.5 46.4 %reduce-scatter.5.cloned.1.call-start = ((), (), s32[]{:S(2)}) async-start(), calls=%async_computation.4 | async-start | bytes 2621440 | tf_op jit(solution)/shard_map/reduce_scatter | solution.py:68
  16.8 69.6 %reduce-scatter.3.cloned.1.call-start = ((), (), s32[]{:S(2)}) async-start(), calls=%async_computation.2 | async-start | bytes 2621440 | tf_op jit(solution)/shard_map/reduce_scatter | solution.py:57
  18.7 34.3 %copy-start.3 = (bf16[4,32,1024]{2,1,0:T(8,128)(2,1)S(1)}, bf16[4,32,1024]{2,1,0:T(8,128)(2,1)}, u32[]{:S(2)}) copy-start(bf16[4,32,1024]{2,1,0:T(8,128)(2,1)} %param.10) | copy-start | bytes 786436
  18.7 70.5 %copy-start.2 = (bf16[32,32,128]{2,1,0:T(8,128)(2,1)S(1)}, bf16[32,32,128]{2,1,0:T(8,128)(2,1)}, u32[]{:S(2)}) copy-start(bf16[32,32,128]{2,1,0:T(8,128)(2,1)} %param.8) | copy-start | bytes 786436
  18.7 94.2 %all-gather.5.cloned.1.call-start = ((), (), s32[]{:S(2)}) async-start(), calls=%async_computation.5 | async-start | bytes 1310720 | tf_op jit(solution)/shard_map/all_gather | solution.py:70
  54.8 86.0 %all-gather.3.cloned.1.call-start = ((), (), s32[]{:S(2)}) async-start(), calls=%async_computation.3 | async-start | bytes 1310720 | tf_op jit(solution)/shard_map/all_gather | solution.py:61
  89.5 1.0 copy-start.1
Sparse Core Ops, SparseCore 0:
  16.9 36.0 reduce-scatter.4
  55.5 30.8 reduce-scatter.2
  88.2 24.6 all-gather.4
  114.6 26.1 all-gather.2
where the time goes:
time: 158 us
  waiting for transfers between devices  109 us (69%)
  matrix products  24.8 us (16%)
  between operations  13.3 us (8%)
  other arithmetic  7.08 us (4%)
  local copies, waits for them, and re-layouts  3.76 us (2%)
    reduce_scatter x1, waiting for transfers between devices, shards(): fwd_z = lax.psum_scatter(partial_z, 'zq', scatter_dimension=0, tiled=True)  34.2 us
    reduce_scatter x1, waiting for transfers between devices, shards(): fwd_y = lax.psum_scatter(partial_y, 'rep', scatter_dimension=0, tiled=True)  31.4 us
    all_gather x1, waiting for transfers between devices, shards(): resid_y = lax.all_gather(resid_y, 'rep', axis=0, tiled=True)  23.7 us
    all_gather x1, waiting for transfers between devices, shards(): resid_z = lax.all_gather(resid_z, 'zq', axis=0, tiled=True)  19.7 us
    dot_general x1, matrix products, shards(): jnp.einsum('sl,zsx->zlx', band_y, resid_y, preferred_element_type=jnp.flo...  10.9 us
    dot_general x1, matrix products, shards(): jnp.einsum('sl,syx->lyx', band_z, resid_z, preferred_element_type=jnp.flo...  4.13 us
  transfers between devices with their start and end apart: 4, of which 4 were waited for; matrix products, arithmetic and copies ran while one was open for 9% of the time, Pallas kernels for 0%

commit v1 on v0

--- a/solution.py
+++ b/solution.py
@@ -58,7 +58,9 @@
     part_z = planes // nrep
     obs_y = lax.dynamic_slice_in_dim(slices_y, rep * part_z, part_z, 0)
     resid_y = (obs_y.astype(jnp.float32) - fwd_y).astype(jnp.bfloat16)
-    resid_y = lax.all_gather(resid_y, "rep", axis=0, tiled=True)
+    resid_y = jnp.concatenate(
+        lax.all_to_all(jnp.stack([resid_y] * lax.axis_size("rep")), "rep", 0, 0), axis=0
+    )
     corr_y = jnp.einsum("sl,zsx->zlx", band_y, resid_y, preferred_element_type=jnp.float32)
     zb = lax.axis_index("zb")
     zq = lax.axis_index("zq")

time: 158 us -> 136 us (0.86); the launches traced: 158 us -> 134 us
  waiting for transfers between devices: 109 us -> 74.1 us
  local copies, waits for them, and re-layouts: 3.76 us -> 7.69 us
  starting transfers between devices: 0.31 us -> 3.91 us
  matrix products: 24.8 us -> 27.2 us
    all_gather x1 -> x0, waiting for transfers between devices: 23.7 us -> none  [shards(): resid_y = lax.all_gather(resid_y, 'rep', axis=0, tiled=True)]
    all_gather x1, waiting for transfers between devices: 19.7 us -> 8.26 us  [shards(): resid_z = lax.all_gather(resid_z, 'zq', axis=0, tiled=True)]
    all_to_all x0 -> x1, starting transfers between devices: none -> 3.82 us  [shards(): lax.all_to_all(jnp.stack([resid_y] * lax.axis_size('rep')), 'rep', 0, 0)]
    convert_element_type x1, local copies, waits for them, and re-layouts: 0.2 us -> 2.03 us  [shards(): slices_x.reshape(planes * rows_here, count_x * SLICES).astype(jnp.float32)]
    dot_general x1, matrix products: 0.83 us -> 2.57 us  [shards(): lax.dot_general(flat_coarse, banded_x, (((1,), (1,)), ((), ())), preferre...]
    convert_element_type x1, other arithmetic: 0.05 us -> 1.78 us  [shards(): slices_x.reshape(planes * rows_here, count_x * SLICES).astype(jnp.float32)]
  transfers between devices with their start and end apart: 4 -> 4, of which waited for: 4 -> 3; matrix products, arithmetic and copies ran while one was open for 9% -> 17% of each run, Pallas kernels for 0% -> 0%
where the time goes in v1:
time: 136 us; the launch traced here: 134 us
  waiting for transfers between devices  74.1 us (54%)
  matrix products  27.2 us (20%)
  between operations  13.2 us (10%)
  other arithmetic  8.16 us (6%)
  local copies, waits for them, and re-layouts  7.69 us (6%)
  starting transfers between devices  3.91 us (3%)
    reduce_scatter x1, waiting for transfers between devices, shards(): fwd_z = lax.psum_scatter(partial_z, 'zq', scatter_dimension=0, tiled=True)  34.2 us
    reduce_scatter x1, waiting for transfers between devices, shards(): fwd_y = lax.psum_scatter(partial_y, 'rep', scatter_dimension=0, tiled=True)  31.6 us
    dot_general x1, matrix products, shards(): jnp.einsum('sl,zsx->zlx', band_y, resid_y, preferred_element_type=jnp.flo...  10.6 us
    all_gather x1, waiting for transfers between devices, shards(): resid_z = lax.all_gather(resid_z, 'zq', axis=0, tiled=True)  8.26 us
    dot_general x1, matrix products, shards(): jnp.einsum('sl,syx->lyx', band_z, resid_z, preferred_element_type=jnp.flo...  4.14 us
    all_to_all x1, starting transfers between devices, shards(): lax.all_to_all(jnp.stack([resid_y] * lax.axis_size('rep')), 'rep', 0, 0)  3.82 us
    dot_general x1, matrix products, shards(): jnp.dot(resid_x, banded_x, preferred_element_type=jnp.float32)  3.68 us
  transfers between devices with their start and end apart: 4, of which 3 were waited for; matrix products, arithmetic and copies ran while one was open for 17% of the time, Pallas kernels for 0%

profile of v1, /device:TPU:1, one launch (start us, length us, event | category | flops | bytes accessed | tf_op | source)
XLA Modules:
  0.0 134.3 jit_solution(3003035407129895689)
XLA Ops:
  6.5 0.7 add_select_fusion
  7.3 1.0 fusion.15
  8.3 1.0 fusion.8
  9.4 2.6 %convert_element_type.40 = bf16[32,32,1024]{2,1,0:T(8,128)(2,1)S(1)} convert(f32[32,32,1024]{2,1,0:T(8,128)} %param.7) | non-fusion elementwise | flops 1048576 | bytes 6291456 | tf_op jit(solution)/shard_map/convert_element_type | solution.py:41
  12.0 2.4 %fusion.3 = f32[16,32,1024]{2,0,1:T(8,128)S(1)} fusion(bf16[32,32,1024]{2,1,0:T(8,128)(2,1)S(1)} %convert_element_type.40, bf16[16,16,128]{2,1,0:T(8,128)(2,1)S(1)} %slice.14, s32[]{:T(128)S(6)} %select_n.32, s32[]{:T(128)S(6)} %select_n.34), kind=kOutput, calls=%fused_computation.4 | convolution fusion | flops 33554432 | bytes 4198408 | tf_op jit(solution)/shard_map/sl,lyx->syx/dot_general | solution.py:69
  14.3 2.5 %copy.21 = f32[16,32,1024]{2,1,0:T(8,128)} copy(f32[16,32,1024]{2,0,1:T(8,128)S(1)} %fusion.3) | data formatting | bytes 4194304 | tf_op jit(solution)/shard_map/sl,lyx->syx/dot_general | solution.py:69
  17.0 1.8 %convolution_bitcast_fusion = f32[32,16,1024]{2,1,0:T(8,128)} fusion(bf16[32,32,1024]{2,1,0:T(8,128)(2,1)S(1)} %convert_element_type.40, bf16[1,16,128]{2,1,0:T(8,128)(2,1)S(1)} %slice.13, s32[]{:T(128)S(6)} %select_n.30), kind=kOutput, calls=%fused_computation.8 | convolution fusion | flops 33554432 | bytes 4198404 | tf_op jit(solution)/shard_map/sl,zlx->zsx/dot_general | solution.py:56
  18.8 0.0 all-gather.2.cloned.1.call-start
  18.9 34.2 %reduce-scatter.5.cloned.1.call-done = f32[4,32,1024]{2,1,0:T(8,128)} async-done(((f32[16,32,1024]{2,1,0:T(8,128)}), f32[4,32,1024]{2,1,0:T(8,128)}) %reduce-scatter.5.cloned.1.call-update) | async-done | bytes 524304 | tf_op jit(solution)/shard_map/reduce_scatter | solution.py:70
  53.1 1.8 %subtract_convert_fusion = bf16[4,32,1024]{2,1,0:T(8,128)(2,1)} fusion(f32[4,32,1024]{2,1,0:T(8,128)} %reduce-scatter.5.cloned.1.call-done, bf16[4,32,1024]{2,1,0:T(8,128)(2,1)S(1)} %copy-done.1), kind=kLoop, calls=%fused_computation.16 | loop fusion | flops 393216 | bytes 1048576 | tf_op jit(solution)/shard_map/convert_element_type | solution.py:71
  54.9 31.6 %reduce-scatter.3.cloned.1.call-done = f32[8,16,1024]{2,1,0:T(8,128)} async-done(((f32[32,16,1024]{2,1,0:T(8,128)}), f32[8,16,1024]{2,1,0:T(8,128)}) %reduce-scatter.3.cloned.1.call-update) | async-done | bytes 524304 | tf_op jit(solution)/shard_map/reduce_scatter | solution.py:57
  86.5 1.2 subtract_convert_fusion.1
  87.7 1.1 stack.2
  88.8 3.8 %all-to-all-start = ((bf16[4,8,16,1024]{3,2,1,0:T(8,128)(2,1)}), bf16[4,8,16,1024]{3,2,1,0:T(8,128)(2,1)S(1)}, u32[]{:S(2)}, u32[]{:S(2)}) async-start(bf16[4,8,16,1024]{3,2,1,0:T(8,128)(2,1)} %stack.2), calls=%async_computation.1 | async-start | bytes 2097152 | tf_op jit(solution)/shard_map/all_to_all | solution.py:62
  92.6 0.1 broadcast_multiply_fusion
  92.7 0.8 reshape.78
  93.6 1.8 %bitcast_convert_fusion = f32[1024,128]{1,0:T(8,128)} fusion(bf16[32,32,128]{2,1,0:T(8,128)(2,1)} %param.8), kind=kLoop, calls=%fused_computation.20 | loop fusion | flops 131072 | bytes 786432 | tf_op jit(solution)/shard_map/convert_element_type | solution.py:48
  95.3 2.0 %copy.18 = f32[1024,128]{0,1:T(8,128)} copy(f32[1024,128]{1,0:T(8,128)} %bitcast_convert_fusion) | data formatting | bytes 1048576 | tf_op jit(solution)/shard_map/convert_element_type | solution.py:48
  97.4 2.6 %fusion.7 = bf16[1024,128]{0,1:T(8,128)(2,1)} fusion(f32[1024,128]{0,1:T(8,128)} %copy.18, bf16[1024,1024]{1,0:T(8,128)(2,1)S(1)} %bitcast.49, bf16[16,8,8,128]{3,2,1,0:T(8,128)(2,1)S(1)} %bitcast.51), kind=kOutput, calls=%fused_computation.11 | convolution fusion | flops 268697600 | bytes 3145728 | tf_op jit(solution)/shard_map/dot_general | solution.py:44
  99.9 1.1 copy.19
  101.1 3.7 %fusion.37 = f32[32,32,1024]{2,1,0:T(8,128)} fusion(bf16[32,32,128]{2,1,0:T(8,128)(2,1)S(1)} %bitcast.52, bf16[128,1024,1]{1,0,2:T(8,128)(2,1)} %reshape.78), kind=kOutput, calls=%fused_computation.49 | convolution fusion | flops 268435456 | bytes 4718592 | tf_op jit(solution)/shard_map/dot_general | solution.py:50
  104.8 8.3 %all-gather.2.cloned.1.call-done = bf16[16,32,1024]{2,1,0:T(8,128)(2,1)} async-done(((bf16[4,32,1024]{2,1,0:T(8,128)(2,1)}), bf16[16,32,1024]{2,1,0:T(8,128)(2,1)}) %all-gather.2.cloned.1.call-update) | async-done | bytes 1048592 | tf_op jit(solution)/shard_map/all_gather | solution.py:72
  113.0 4.1 %fusion.9 = f32[32,32,1024]{2,0,1:T(8,128)} fusion(bf16[16,32,1024]{2,1,0:T(8,128)(2,1)} %all-gather.2.cloned.1.call-done, bf16[16,16,128]{2,1,0:T(8,128)(2,1)} %copy-done.3, s32[]{:T(128)S(6)} %select_n.32, s32[]{:T(128)S(6)} %select_n.34), kind=kOutput, calls=%fused_computation.13 | convolution fusion | flops 33554432 | bytes 5246984 | tf_op jit(solution)/shard_map/sl,syx->lyx/dot_general | solution.py:73
  117.2 10.6 %fusion.2 = f32[32,32,1024]{2,1,0:T(8,128)} fusion(f32[32,32,1024]{2,1,0:T(8,128)} %param.7, f32[32,32,1024]{2,1,0:T(8,128)} %fusion.37, f32[32,32,1024]{2,0,1:T(8,128)} %fusion.9, bf16[32,16,1024]{2,1,0:T(8,128)(2,1)S(1)} %bitcast.50, bf16[1,16,128]{2,1,0:T(8,128)(2,1)S(1)} %slice.13, s32[]{:T(128)S(6)} %select_n.30), kind=kOutput, calls=%fused_computation.3 | convolution fusion | flops 37748736 | bytes 17829892 | tf_op jit(solution)/shard_map/sl,zsx->zlx/dot_general | solution.py:64
  (19 shorter events, 0.1 us)
Async XLA Ops:
  6.5 0.8 copy-start
  6.5 46.5 %reduce-scatter.5.cloned.1.call-start = ((), (), s32[]{:S(2)}) async-start(), calls=%async_computation.4 | async-start | bytes 2621440 | tf_op jit(solution)/shard_map/reduce_scatter | solution.py:70
  9.3 45.6 %copy-start.2 = (bf16[25,16,128]{2,1,0:T(8,128)(2,1)}, bf16[25,16,128]{2,1,0:T(8,128)(2,1)S(1)}, u32[]{:S(2)}) copy-start(bf16[25,16,128]{2,1,0:T(8,128)(2,1)S(1)} %fusion.8) | copy-start | bytes 307204
  9.4 2.6 %copy-start.3 = (bf16[16,16,128]{2,1,0:T(8,128)(2,1)}, bf16[16,16,128]{2,1,0:T(8,128)(2,1)S(1)}, u32[]{:S(2)}) copy-start(bf16[16,16,128]{2,1,0:T(8,128)(2,1)S(1)} %slice.14) | copy-start | bytes 196612
  16.9 69.6 %reduce-scatter.3.cloned.1.call-start = ((), (), s32[]{:S(2)}) async-start(), calls=%async_computation.3 | async-start | bytes 2621440 | tf_op jit(solution)/shard_map/reduce_scatter | solution.py:57
  18.8 34.3 %copy-start.1 = (bf16[4,32,1024]{2,1,0:T(8,128)(2,1)S(1)}, bf16[4,32,1024]{2,1,0:T(8,128)(2,1)}, u32[]{:S(2)}) copy-start(bf16[4,32,1024]{2,1,0:T(8,128)(2,1)} %param.10) | copy-start | bytes 786436
  18.8 94.2 %all-gather.2.cloned.1.call-start = ((), (), s32[]{:S(2)}) async-start(), calls=%async_computation.5 | async-start | bytes 1310720 | tf_op jit(solution)/shard_map/all_gather | solution.py:72
  54.9 37.7 %slice-start = ((bf16[25,16,128]{2,1,0:T(8,128)(2,1)}), bf16[8,16,128]{2,1,0:T(8,128)(2,1)S(1)}, s32[]{:S(2)}) async-start(bf16[25,16,128]{2,1,0:T(8,128)(2,1)} %copy-done.2), calls=%async_computation.6 | async-start | bytes 65536 | tf_op jit(solution)/shard_map/slice | solution.py:38
  88.8 28.4 %all-to-all-start = ((bf16[4,8,16,1024]{3,2,1,0:T(8,128)(2,1)}), bf16[4,8,16,1024]{3,2,1,0:T(8,128)(2,1)S(1)}, u32[]{:S(2)}, u32[]{:S(2)}) async-start(bf16[4,8,16,1024]{3,2,1,0:T(8,128)(2,1)} %stack.2), calls=%async_computation.1 | async-start | bytes 2097152 | tf_op jit(solution)/shard_map/all_to_all | solution.py:62
Sparse Core Ops, SparseCore 0:
  17.0 36.0 reduce-scatter.4
  55.6 30.8 reduce-scatter.2
  88.3 24.6 all-gather.1
